TPU v7x, 128 devices: a whole 4x4x4 slice. The times are simulated.
128 devices in a mesh: half: 2 (over core), row: 8 (over z_hi, x), col: 8 (over y, z_lo).
Axes of the slice: x: 4, y: 4, z: 4 (z_hi: 2, z_lo: 2; z = z_hi * 2 + z_lo), core: 2. Of those that a mesh axis runs over, the one named last changes fastest.
Arguments:
- child_diag: float32 [2, 512, 512], P('half'), as said below
- child_panel: float32 [2, 16, 8, 128, 512], P('half', None, 'row'), may hold values from -18 to 18
- child_window: float32 [2, 16, 8, 128, 8, 8, 128], P('half', None, 'row', None, None, 'col'), may hold values from -6 to 6
- parent_diag: float32 [512, 512], replicated
- parent_lead_panel: float32 [24, 8, 2, 8, 8, 512], P(None, 'row', 'half', 'col'), may hold values from -24 to 24
- index_maps: int32 [2, 128], replicated, may hold values from 0 to 191, as said below
Outputs:
- parent_front: float32 [24, 8, 128, 4, 2, 8, 128], P(None, 'row', None, None, 'half', 'col')
- parent_factor: float32 [24, 8, 2, 8, 8, 512], P(None, 'row', 'half', 'col')
- parent_pivot: float32 [512, 512], replicated
Inputs may be any that keep to these rules, and one draw needn't show every extreme that they name: child_diag and parent_diag are symmetric and positive definite. For each child k and each group a, the entries index_maps[k, a * 16 + u] with 0 <= u < 16 equal q * 16 + ((u + s) mod 16) for a group target q and a turn s fixed within the group; groups a < 4 have q = a, later groups have distinct q that rise with a; over the 8 groups of a child the turns s, taken modulo 8, are all different; for each child some group a < 4 has a turn divisible by 8, and another group a < 4 has a turn that leaves 1 modulo 8.
All inputs are finite; a program needn't handle non-finite values.
Results may differ from a plain program's by a relative error of at most 0.0001.
Values sent between devices are 32-bit elements; how exact they have to be, the bound alone decides.
No kernel may reach another device: no remote copies, remote signals or barrier semaphores. Data moves between devices by JAX's collectives and lax.ppermute only.
A program may use at most 192 MiB of HBM per device.

v0:
```python
import jax
import jax.numpy as jnp
from jax import lax
from jax.sharding import PartitionSpec as P

BLOCK_EXTENT = 128
PB = 4
SB = 128
RB = 192
WB = 64


def from_root(shard, axis, root):
    mine = lax.axis_index(axis) == root
    return lax.psum(jnp.where(mine, shard, jnp.zeros_like(shard)), axis)


def pick_ranked(owners, values, wanted, slot_count, missing):
    matches = owners[..., None, :] == wanted[:, None]
    ranking = jnp.cumsum(matches.astype(jnp.int32), axis=-1) - 1
    slot_ids = jnp.arange(slot_count, dtype=jnp.int32)
    chosen = matches[..., None, :] & (ranking[..., None, :] == slot_ids[:, None])
    present = jnp.any(chosen, axis=-1)
    picked = jnp.sum(jnp.where(chosen, values[..., None, None, :], 0), axis=-1)
    return jnp.where(present, picked, missing)


def per_device(child_diag, child_panel, child_window, parent_diag, parent_lead_panel, index_maps):
    highest = lax.Precision.HIGHEST
    row_size = lax.axis_size("row")
    half_id = lax.axis_index("half")
    row_id = lax.axis_index("row")
    col_id = lax.axis_index("col")
    panel_width = PB * BLOCK_EXTENT
    group_size = 2 * row_size
    row_local = SB // row_size
    col_local = WB // row_size
    parent_row_blocks = RB // row_size
    parent_cols = WB // group_size
    per_row = 2 * (SB // group_size) // row_size
    per_col = (WB // group_size + row_size - 1) // row_size
    pivot_lower_factor = jnp.linalg.cholesky(parent_diag)
    own_rows = parent_lead_panel.reshape(-1, panel_width)
    solved = jax.scipy.linalg.solve_triangular(pivot_lower_factor, own_rows.T, lower=True).T
    parent_factor = solved.reshape(parent_lead_panel.shape)
    sub_rows = parent_lead_panel.shape[4]
    gathered = lax.all_gather(
        solved.reshape(parent_row_blocks, sub_rows, panel_width),
        ("half", "col"),
        axis=1,
        tiled=True,
    )
    paired = gathered[: 2 * parent_cols].reshape(parent_cols, 2, BLOCK_EXTENT, panel_width)
    offered = lax.dynamic_index_in_dim(paired, half_id, axis=1, keepdims=False)
    column_factor = from_root(offered, "row", col_id)
    child_low = jnp.linalg.cholesky(child_diag[0])
    child_rows = child_panel.reshape(-1, panel_width)
    child_factor = jax.scipy.linalg.solve_triangular(child_low, child_rows.T, lower=True).T
    leading = child_factor[: col_local * BLOCK_EXTENT]
    everyone = lax.all_gather(leading[None], "row", axis=0, tiled=True)
    child_columns = lax.dynamic_index_in_dim(everyone, col_id, axis=0, keepdims=False)
    schur_part = child_window.reshape(row_local * BLOCK_EXTENT, col_local * BLOCK_EXTENT) - jnp.dot(
        child_factor, child_columns.T, precision=highest
    )
    schur_blocks = schur_part.reshape(row_local, BLOCK_EXTENT, col_local, BLOCK_EXTENT)
    child_map = lax.dynamic_index_in_dim(index_maps, half_id, axis=0, keepdims=False)
    my_rows = lax.dynamic_index_in_dim(
        child_map.reshape(row_local, row_size), row_id, axis=1, keepdims=False
    )
    my_cols = lax.dynamic_index_in_dim(
        child_map[:WB].reshape(col_local, row_size), col_id, axis=1, keepdims=False
    )
    local_rows = jnp.arange(row_local, dtype=jnp.int32)
    local_cols = jnp.arange(col_local, dtype=jnp.int32)
    send_rows = pick_ranked(
        my_rows % row_size, local_rows, jnp.arange(row_size, dtype=jnp.int32), per_row, row_local
    )
    send_cols = pick_ranked(
        my_cols % group_size,
        local_cols,
        jnp.arange(group_size, dtype=jnp.int32),
        per_col,
        col_local,
    )
    all_rows = index_maps.reshape(2, row_local, row_size).transpose(0, 2, 1)
    row_target = pick_ranked(
        all_rows % row_size, all_rows // row_size, row_id[None], per_row, parent_row_blocks
    )[:, :, 0, :]
    all_cols = index_maps[:, :WB].reshape(2, col_local, row_size).transpose(0, 2, 1)
    col_target = pick_ranked(
        all_cols % group_size,
        all_cols // group_size,
        (half_id * row_size + col_id)[None],
        per_col,
        parent_cols,
    )[:, :, 0, :]
    assembled_front = jnp.zeros(
        (parent_row_blocks, BLOCK_EXTENT, parent_cols, BLOCK_EXTENT), jnp.float32
    )
    row_index = send_rows[None, :, None, :, None]
    col_index = send_cols.reshape(2, row_size, per_col)[:, None, :, None, :]
    outgoing = schur_blocks.at[row_index, :, col_index, :].get(mode="fill", fill_value=0.0)
    arrived = lax.all_to_all(
        outgoing.reshape(-1, per_row * per_col, BLOCK_EXTENT, BLOCK_EXTENT),
        ("half", "row", "col"),
        split_axis=0,
        concat_axis=0,
        tiled=True,
    )
    arrived = arrived.reshape(2, row_size, row_size, per_row, per_col, BLOCK_EXTENT, BLOCK_EXTENT)
    target_rows = row_target[:, :, None, :, None]
    target_cols = col_target[:, None, :, None, :]
    assembled_front = assembled_front.at[target_rows, :, target_cols, :].add(arrived, mode="drop")
    flat_front = assembled_front.reshape(
        parent_row_blocks * BLOCK_EXTENT, parent_cols * BLOCK_EXTENT
    )
    updated = flat_front - jnp.dot(
        gathered.reshape(-1, panel_width),
        column_factor.reshape(-1, panel_width).T,
        precision=highest,
    )
    return (
        updated.reshape(parent_row_blocks, 1, BLOCK_EXTENT, parent_cols, 1, 1, BLOCK_EXTENT),
        parent_factor,
        pivot_lower_factor,
    )


def solution(mesh):
    in_specs = (
        P("half", None, None),
        P("half", None, "row", None, None),
        P("half", None, "row", None, None, "col", None),
        P(),
        P(None, "row", "half", "col", None, None),
        P(),
    )
    out_specs = (
        P(None, "row", None, None, "half", "col", None),
        P(None, "row", "half", "col", None, None),
        P(),
    )
    return jax.shard_map(
        per_device, mesh=mesh, in_specs=in_specs, out_specs=out_specs, check_vma=False
    )
```

profile of v0, /device:TPU:10, one launch (start us, length us, event | category | flops | bytes accessed | tf_op | source)
XLA Modules:
  0.0 815.9 jit_solution(16038382859682363218)
XLA Ops:
  14.1 11.7 %cholesky.286 = f32[128,128]{1,0:T(8,128)S(1)} custom-call(f32[128,128]{1,0:T(8,128)S(1)} %cholesky.426), custom_call_target="Cholesky" | custom-call | tf_op jit(solution)/shard_map/jit(cholesky)/cholesky | solution.py:56
  26.0 9.8 %custom-call.37 = f32[1,128,128]{1,2,0:T(8,128)S(1)} custom-call(f32[1,128,128]{2,1,0:T(8,128)S(1)} %get-tuple-element.91), custom_call_target="InvertDiagBlocksLowerTriangular" | custom-call | tf_op jit(solution)/shard_map/jit(cholesky)/cholesky | solution.py:56
  36.5 11.7 %cholesky.305 = f32[128,128]{1,0:T(8,128)S(1)} custom-call(f32[128,128]{1,0:T(8,128)S(1)} %cholesky.430), custom_call_target="Cholesky" | custom-call | tf_op jit(solution)/shard_map/jit(cholesky)/cholesky | solution.py:56
  48.2 10.2 %custom-call.38 = f32[1,128,128]{1,2,0:T(8,128)S(1)} custom-call(f32[1,128,128]{2,1,0:T(8,128)S(1)} %get-tuple-element.88), custom_call_target="InvertDiagBlocksLowerTriangular" | custom-call | tf_op jit(solution)/shard_map/jit(cholesky)/cholesky | solution.py:56
  59.1 11.7 %cholesky.326 = f32[128,128]{1,0:T(8,128)S(1)} custom-call(f32[128,128]{1,0:T(8,128)S(1)} %cholesky.435), custom_call_target="Cholesky" | custom-call | tf_op jit(solution)/shard_map/jit(cholesky)/cholesky | solution.py:56
  70.9 9.8 %custom-call.39 = f32[1,128,128]{1,2,0:T(8,128)S(1)} custom-call(f32[1,128,128]{2,1,0:T(8,128)S(1)} %get-tuple-element.85), custom_call_target="InvertDiagBlocksLowerTriangular" | custom-call | tf_op jit(solution)/shard_map/jit(cholesky)/cholesky | solution.py:56
  81.3 11.7 %cholesky.343 = f32[128,128]{1,0:T(8,128)S(1)} custom-call(f32[128,128]{1,0:T(8,128)S(1)} %convolution_subtract_fusion.10), custom_call_target="Cholesky" | custom-call | tf_op jit(solution)/shard_map/jit(cholesky)/cholesky | solution.py:56
  106.4 39.3 %custom-call.28 = f32[4,128,128]{1,2,0:T(8,128)S(1)} custom-call(f32[4,128,128]{2,1,0:T(8,128)S(1)} %get-tuple-element.11), custom_call_target="InvertDiagBlocksLowerTriangular" | custom-call | tf_op jit(solution)/shard_map/jit(_solve_triangular)/triangular_solve | solution.py:58
  169.6 11.9 %cholesky.358 = f32[128,128]{1,0:T(8,128)S(1)} custom-call(f32[128,128]{1,0:T(8,128)S(1)} %cholesky.439), custom_call_target="Cholesky" | custom-call | tf_op jit(solution)/shard_map/jit(cholesky)/cholesky | solution.py:42
  195.7 11.7 %cholesky.377 = f32[128,128]{1,0:T(8,128)S(1)} custom-call(f32[128,128]{1,0:T(8,128)S(1)} %cholesky.443), custom_call_target="Cholesky" | custom-call | tf_op jit(solution)/shard_map/jit(cholesky)/cholesky | solution.py:42
  220.2 12.1 %cholesky.398 = f32[128,128]{1,0:T(8,128)S(1)} custom-call(f32[128,128]{1,0:T(8,128)S(1)} %cholesky.448), custom_call_target="Cholesky" | custom-call | tf_op jit(solution)/shard_map/jit(cholesky)/cholesky | solution.py:42
  245.1 11.7 %cholesky.415 = f32[128,128]{1,0:T(8,128)S(1)} custom-call(f32[128,128]{1,0:T(8,128)S(1)} %convolution_subtract_fusion.9), custom_call_target="Cholesky" | custom-call | tf_op jit(solution)/shard_map/jit(cholesky)/cholesky | solution.py:42
  260.6 87.6 %all-gather.6.cloned.1.call-done = f32[8192,512]{0,1:T(8,128)} async-done(((f32[1024,512]{0,1:T(8,128)}), f32[8192,512]{0,1:T(8,128)}) %all-gather.6.cloned.1.call-update) | async-done | bytes 16777232 | tf_op jit(solution)/shard_map/all_gather | solution.py:60
  348.2 21.3 %copy.78 = f32[64,8,8,1024]{3,2,1,0:T(8,128)} copy(f32[64,8,8,1024]{3,1,2,0:T(8,128)} %bitcast.224) | data formatting | bytes 33554432
  378.9 20.5 %fusion = f32[256,8,8,128]{3,1,2,0:T(8,128)S(1)} fusion(f32[256,8,8,128]{3,2,1,0:T(8,128)} %bitcast.231, f32[128,2048]{1,0:T(8,128)} %copy-done.1, f32[128,2048]{1,0:T(8,128)S(1)} %fusion.56, f32[128,2048]{1,0:T(8,128)S(1)} %fusion.58, f32[128,2048]{1,0:T(8,128)S(1)} %fusion.16, f32[1,1024,512]{1,0,2:T(1,128)} %constant_dynamic-slice_fusion.2), kind=kOutput, calls=%fused_computation.7 | convolution fusion | flops 12890144768 | bytes 23068672 | tf_op jit(solution)/shard_map/dot_general | solution.py:62
  406.3 16.0 %gather_fusion = f32[256,128,128]{2,1,0:T(8,128)} fusion(f32[16,128,8,128]{3,1,2,0:T(8,128)} %copy.67, s32[256]{0:T(256)S(1)} %reshape.575), kind=kCustom, calls=%fused_computation | custom fusion | bytes 33556480 | tf_op jit(solution)/shard_map/gather | solution.py:102
  422.3 11.4 %broadcast_select_fusion = f32[128,2,128,128]{3,2,1,0:T(8,128)} fusion(f32[128,2,128,128]{3,2,1,0:T(8,128)} %bitcast.220, pred[128,2]{1,0:T(8,128)(4,1)S(1)} %bitcast.239), kind=kLoop, calls=%fused_computation.8 | loop fusion | flops 4194304 | bytes 33554688 | tf_op jit(solution)/shard_map/select_n | solution.py:102
  452.2 39.3 %custom-call.29 = f32[4,128,128]{1,2,0:T(8,128)S(1)} custom-call(f32[4,128,128]{2,1,0:T(8,128)S(1)} %get-tuple-element.19), custom_call_target="InvertDiagBlocksLowerTriangular" | custom-call | tf_op jit(solution)/shard_map/jit(_solve_triangular)/triangular_solve | solution.py:44
  494.7 187.4 %all-gather.4.cloned.1.call-done = f32[24,128,512]{2,1,0:T(8,128)} async-done(((f32[24,8,512]{2,1,0:T(8,128)}), f32[24,128,512]{2,1,0:T(8,128)}) %all-gather.4.cloned.1.call-update) | async-done | bytes 6291472 | tf_op jit(solution)/shard_map/all_gather | solution.py:47
  685.9 18.8 %all-to-all-done = f32[128,2,128,128]{3,2,1,0:T(8,128)} async-done(((f32[128,2,128,128]{3,2,1,0:T(8,128)}), f32[128,2,128,128]{3,2,1,0:T(8,128)}, u32[]{:S(2)}, u32[]{:S(2)}) %all-to-all-start) | async-done | bytes 16777248 | tf_op jit(solution)/shard_map/all_to_all | solution.py:103
  708.2 51.7 %scatter_fusion = f32[24,128,4,128]{3,1,2,0:T(8,128)} fusion(f32[24,128,4,128]{3,1,2,0:T(8,128)} %broadcast_in_dim.109, s32[256]{0:T(256)S(1)} %reshape.583, f32[256,128,128]{2,1,0:T(8,128)} %bitcast.23), kind=kCustom, calls=%fused_computation.1 | custom fusion | flops 4194304 | bytes 50333696 | tf_op jit(solution)/shard_map/scatter-add | solution.py:113
  760.0 10.4 %copy.68 = f32[24,128,4,128]{3,2,1,0:T(4,128)} copy(f32[24,128,4,128]{3,1,2,0:T(8,128)} %scatter_fusion) | data formatting | bytes 12582912 | tf_op jit(solution)/shard_map/scatter-add | solution.py:113
  770.4 14.2 %all-reduce.3.cloned.1.call-done = f32[512,512]{1,0:T(8,128)} async-done(((f32[512,512]{1,0:T(8,128)}), f32[512,512]{1,0:T(8,128)}) %all-reduce.3.cloned.1.call-update) | async-done | bytes 1048592 | tf_op jit(solution)/shard_map/psum | solution.py:15
  784.6 16.1 %bitcast_subtract_fusion.1 = f32[3072,512]{1,0:T(8,128)} fusion(f32[384,8,4,128]{3,2,1,0:T(4,128)} %bitcast.222, f32[3072,512]{1,0:T(8,128)} %bitcast.229, f32[512,512]{1,0:T(8,128)} %all-reduce.3.cloned.1.call-done), kind=kOutput, calls=%fused_computation.9 | convolution fusion | flops 9665249280 | bytes 19922944 | tf_op jit(solution)/shard_map/dot_general | solution.py:117
  (173 shorter events, 152.6 us)
Async XLA Ops:
  8.0 340.2 %all-gather.6.cloned.1.call-start = ((), (), s32[]{:S(2)}) async-start(), calls=%async_computation.3 | async-start | bytes 18874368 | tf_op jit(solution)/shard_map/all_gather | solution.py:60
  8.1 5.4 copy-start.3
  106.4 45.1 %copy-start.4 = (f32[512,512]{1,0:T(8,128)}, f32[512,512]{1,0:T(8,128)S(1)}, u32[]{:S(2)}) copy-start(f32[512,512]{1,0:T(8,128)S(1)} %get-tuple-element.206) | copy-start | bytes 3145732
  145.7 5.7 copy-start
  157.9 1.0 copy-start.1
  159.1 2.1 copy-start.7
  159.2 4.8 copy-start.8
  168.6 1.0 copy-start.5
  433.6 8.8 %copy-start.2 = (f32[512,512]{1,0:T(8,128)S(1)}, f32[512,512]{1,0:T(8,128)}, u32[]{:S(2)}) copy-start(f32[512,512]{1,0:T(8,128)} %get-tuple-element.73) | copy-start | bytes 3145732
  433.6 271.1 %all-to-all-start = ((f32[128,2,128,128]{3,2,1,0:T(8,128)}), f32[128,2,128,128]{3,2,1,0:T(8,128)}, u32[]{:S(2)}, u32[]{:S(2)}) async-start(f32[128,2,128,128]{3,2,1,0:T(8,128)} %broadcast_select_fusion), calls=%async_computation | async-start | bytes 33554432 | tf_op jit(solution)/shard_map/all_to_all | solution.py:103
  441.1 50.4 %copy-start.6 = (f32[24,1,1,1,8,512]{5,4,3,2,1,0:T(8,128)S(1)}, f32[24,1,1,1,8,512]{5,4,3,2,1,0:T(8,128)}, u32[]{:S(2)}) copy-start(f32[24,1,1,1,8,512]{5,4,3,2,1,0:T(8,128)} %param.11) | copy-start | bytes 1179652
  441.1 241.0 %all-gather.4.cloned.1.call-start = ((), (), s32[]{:S(2)}) async-start(), calls=%async_computation.1 | async-start | bytes 6684672 | tf_op jit(solution)/shard_map/all_gather | solution.py:47
  494.5 290.2 %all-reduce.3.cloned.1.call-start = ((), (), s32[]{:S(2)}) async-start(), calls=%async_computation.2 | async-start | bytes 2097152 | tf_op jit(solution)/shard_map/psum | solution.py:15
  682.1 1.6 slice-start
Sparse Core Ops, SparseCore 0:
  160.9 187.2 all-gather.5
  684.9 99.7 all-reduce.2
Sparse Core Ops, SparseCore 1:
  494.6 187.5 all-gather.3
where the time goes:
time: 830 us; the launch traced here: 816 us
  other arithmetic  309 us (37%)
  waiting for transfers between devices  308 us (37%)
  local copies, waits for them, and re-layouts  109 us (13%)
  matrix products  60.3 us (7%)
  between operations  21.3 us (3%)
    all_gather x1, waiting for transfers between devices, per_device(): lax.all_gather(solved.reshape(parent_row_blocks, sub_rows, panel_width),...  187 us
    all_gather x1, waiting for transfers between devices, per_device(): everyone = lax.all_gather(leading[None], 'row', axis=0, tiled=True)  87.6 us
    another operation x14, other arithmetic, per_device(): pivot_lower_factor = jnp.linalg.cholesky(parent_diag)  80.7 us
    another operation x14, other arithmetic, per_device(): child_low = jnp.linalg.cholesky(child_diag[0])  78.9 us
    scatter-add x1, other arithmetic, per_device(): assembled_front.at[target_rows, :, target_cols, :].add(arrived, mode='drop')  51.7 us
    another operation x2, other arithmetic, per_device(): jax.scipy.linalg.solve_triangular(pivot_lower_factor, own_rows.T, lower=T...  40.6 us
    another operation x3, other arithmetic, per_device(): jax.scipy.linalg.solve_triangular(child_low, child_rows.T, lower=True)  39.4 us
    unnamed x24, local copies, waits for them, and re-layouts  28.3 us
  transfers between devices with their start and end apart: 4, of which 4 were waited for; matrix products, arithmetic and copies ran while one was open for 27% of the time, Pallas kernels for 0%

commit v1 on v0

--- a/solution.py
+++ b/solution.py
@@ -28,6 +28,7 @@
 def per_device(child_diag, child_panel, child_window, parent_diag, parent_lead_panel, index_maps):
     highest = lax.Precision.HIGHEST
     row_size = lax.axis_size("row")
+    col_size = lax.axis_size("col")
     half_id = lax.axis_index("half")
     row_id = lax.axis_index("row")
     col_id = lax.axis_index("col")
@@ -39,30 +40,42 @@
     parent_cols = WB // group_size
     per_row = 2 * (SB // group_size) // row_size
     per_col = (WB // group_size + row_size - 1) // row_size
-    pivot_lower_factor = jnp.linalg.cholesky(parent_diag)
+    transpose_perm = [(i * col_size + j, j * row_size + i) for i in range(row_size) for j in range(col_size)]
+    child_lead = child_panel[0, :col_local, 0]
+    child_col_rows = lax.ppermute(child_lead, ("row", "col"), transpose_perm)
+    sub_rows = parent_lead_panel.shape[4]
     own_rows = parent_lead_panel.reshape(-1, panel_width)
-    solved = jax.scipy.linalg.solve_triangular(pivot_lower_factor, own_rows.T, lower=True).T
-    parent_factor = solved.reshape(parent_lead_panel.shape)
-    sub_rows = parent_lead_panel.shape[4]
     gathered = lax.all_gather(
-        solved.reshape(parent_row_blocks, sub_rows, panel_width),
+        parent_lead_panel.reshape(parent_row_blocks, sub_rows, panel_width),
         ("half", "col"),
         axis=1,
         tiled=True,
     )
     paired = gathered[: 2 * parent_cols].reshape(parent_cols, 2, BLOCK_EXTENT, panel_width)
     offered = lax.dynamic_index_in_dim(paired, half_id, axis=1, keepdims=False)
-    column_factor = from_root(offered, "row", col_id)
+    parent_col_rows = lax.ppermute(offered, ("row", "col"), transpose_perm)
+    eye = jnp.eye(panel_width, dtype=jnp.float32)
     child_low = jnp.linalg.cholesky(child_diag[0])
+    child_inv = lax.linalg.triangular_solve(child_low, eye, left_side=True, lower=True)
     child_rows = child_panel.reshape(-1, panel_width)
-    child_factor = jax.scipy.linalg.solve_triangular(child_low, child_rows.T, lower=True).T
-    leading = child_factor[: col_local * BLOCK_EXTENT]
-    everyone = lax.all_gather(leading[None], "row", axis=0, tiled=True)
-    child_columns = lax.dynamic_index_in_dim(everyone, col_id, axis=0, keepdims=False)
-    schur_part = child_window.reshape(row_local * BLOCK_EXTENT, col_local * BLOCK_EXTENT) - jnp.dot(
-        child_factor, child_columns.T, precision=highest
+    dims = (((1,), (1,)), ((), ()))
+    child_factor = lax.dot_general(child_rows, child_inv, dims, precision=highest)
+    child_columns = lax.dot_general(
+        child_col_rows.reshape(-1, panel_width), child_inv, dims, precision=highest
+    )
+    schur_part = child_window.reshape(row_local * BLOCK_EXTENT, col_local * BLOCK_EXTENT) - lax.dot_general(
+        child_factor, child_columns, dims, precision=highest
     )
     schur_blocks = schur_part.reshape(row_local, BLOCK_EXTENT, col_local, BLOCK_EXTENT)
+    pivot_lower_factor = jnp.linalg.cholesky(parent_diag)
+    parent_inv = lax.linalg.triangular_solve(pivot_lower_factor, eye, left_side=True, lower=True)
+    solved = lax.dot_general(own_rows, parent_inv, dims, precision=highest)
+    parent_factor = solved.reshape(parent_lead_panel.shape)
+    row_factor = lax.dot_general(gathered.reshape(-1, panel_width), parent_inv, dims, precision=highest)
+    column_factor = lax.dot_general(
+        parent_col_rows.reshape(-1, panel_width), parent_inv, dims, precision=highest
+    )
+    update = lax.dot_general(row_factor, column_factor, dims, precision=highest)
     child_map = lax.dynamic_index_in_dim(index_maps, half_id, axis=0, keepdims=False)
     my_rows = lax.dynamic_index_in_dim(
         child_map.reshape(row_local, row_size), row_id, axis=1, keepdims=False
@@ -114,11 +127,7 @@
     flat_front = assembled_front.reshape(
         parent_row_blocks * BLOCK_EXTENT, parent_cols * BLOCK_EXTENT
     )
-    updated = flat_front - jnp.dot(
-        gathered.reshape(-1, panel_width),
-        column_factor.reshape(-1, panel_width).T,
-        precision=highest,
-    )
+    updated = flat_front - update
     return (
         updated.reshape(parent_row_blocks, 1, BLOCK_EXTENT, parent_cols, 1, 1, BLOCK_EXTENT),
         parent_factor,

time: 830 us -> 690 us (0.83)
  waiting for transfers between devices: 308 us -> 159 us
  local copies, waits for them, and re-layouts: 109 us -> 71.3 us
  matrix products: 60.3 us -> 88.5 us
  starting transfers between devices: 7.56 us -> 29.6 us
    all_gather x2 -> x1, waiting for transfers between devices: 275 us -> 115 us  [per_device(): lax.all_gather(parent_lead_panel.reshape(parent_row_blocks, sub_rows, pan...]
    ppermute x0 -> x2, waiting for transfers between devices: none -> 43 us  [the longest x1 43 us: per_device(): parent_col_rows = lax.ppermute(offered, ('row', 'col'), transpose_perm)]
    dot_general x2 -> x7, matrix products: 36.6 us -> 70.5 us  [the longest x1 23 us: per_device(): update = lax.dot_general(row_factor, column_factor, dims, precision=highest)]
    unnamed x24 -> x23, local copies, waits for them, and re-layouts: 28.3 us -> 5.94 us
    all_to_all x1, waiting for transfers between devices: 18.8 us -> 0.01 us  [per_device(): lax.all_to_all(outgoing.reshape(-1, per_row * per_col, BLOCK_EXTENT, BLOC...]
    all_to_all x1, starting transfers between devices: 7.44 us -> 23 us  [per_device(): lax.all_to_all(outgoing.reshape(-1, per_row * per_col, BLOCK_EXTENT, BLOC...]
    psum x1 -> x0, waiting for transfers between devices: 14.2 us -> none  [from_root(): return lax.psum(jnp.where(mine, shard, jnp.zeros_like(shard)), axis)]
    another operation x14, other arithmetic: 78.9 us -> 89.1 us  [per_device(): child_low = jnp.linalg.cholesky(child_diag[0])]
  transfers between devices with their start and end apart: 4 -> 4, of which waited for: 4 -> 2; matrix products, arithmetic and copies ran while one was open for 27% -> 47% of each run, Pallas kernels for 0% -> 0%
where the time goes in v1:
time: 690 us; the launch traced here: 682 us
  other arithmetic  314 us (46%)
  waiting for transfers between devices  159 us (23%)
  matrix products  88.5 us (13%)
  local copies, waits for them, and re-layouts  71.3 us (10%)
  starting transfers between devices  29.6 us (4%)
  between operations  20 us (3%)
    all_gather x1, waiting for transfers between devices, per_device(): lax.all_gather(parent_lead_panel.reshape(parent_row_blocks, sub_rows, pan...  115 us
    another operation x14, other arithmetic, per_device(): child_low = jnp.linalg.cholesky(child_diag[0])  89.1 us
    another operation x14, other arithmetic, per_device(): pivot_lower_factor = jnp.linalg.cholesky(parent_diag)  78.5 us
    scatter-add x1, other arithmetic, per_device(): assembled_front.at[target_rows, :, target_cols, :].add(arrived, mode='drop')  51.7 us
    ppermute x1, waiting for transfers between devices, per_device(): parent_col_rows = lax.ppermute(offered, ('row', 'col'), transpose_perm)  43 us
    another operation x2, other arithmetic, per_device(): lax.linalg.triangular_solve(pivot_lower_factor, eye, left_side=True, lowe...  40.8 us
    another operation x3, other arithmetic, per_device(): lax.linalg.triangular_solve(child_low, eye, left_side=True, lower=True)  39.4 us
    dot_general x1, matrix products, per_device(): update = lax.dot_general(row_factor, column_factor, dims, precision=highest)  23 us
  transfers between devices with their start and end apart: 4, of which 2 were waited for; matrix products, arithmetic and copies ran while one was open for 47% of the time, Pallas kernels for 0%

profile of v1, /device:TPU:10, one launch (start us, length us, event | category | flops | bytes accessed | tf_op | source)
XLA Modules:
  0.0 682.1 jit_solution(13045459149340922864)
XLA Ops:
  22.0 11.7 %cholesky.286 = f32[128,128]{1,0:T(8,128)S(1)} custom-call(f32[128,128]{1,0:T(8,128)S(1)} %cholesky.426), custom_call_target="Cholesky" | custom-call | tf_op jit(solution)/shard_map/jit(cholesky)/cholesky | solution.py:58
  33.9 9.8 %custom-call.31 = f32[1,128,128]{1,2,0:T(8,128)S(1)} custom-call(f32[1,128,128]{2,1,0:T(8,128)S(1)} %get-tuple-element.90), custom_call_target="InvertDiagBlocksLowerTriangular" | custom-call | tf_op jit(solution)/shard_map/jit(cholesky)/cholesky | solution.py:58
  46.2 11.7 %cholesky.305 = f32[128,128]{1,0:T(8,128)S(1)} custom-call(f32[128,128]{1,0:T(8,128)S(1)} %cholesky.430), custom_call_target="Cholesky" | custom-call | tf_op jit(solution)/shard_map/jit(cholesky)/cholesky | solution.py:58
  58.0 10.0 %custom-call.32 = f32[1,128,128]{1,2,0:T(8,128)S(1)} custom-call(f32[1,128,128]{2,1,0:T(8,128)S(1)} %get-tuple-element.87), custom_call_target="InvertDiagBlocksLowerTriangular" | custom-call | tf_op jit(solution)/shard_map/jit(cholesky)/cholesky | solution.py:58
  69.6 11.7 %cholesky.326 = f32[128,128]{1,0:T(8,128)S(1)} custom-call(f32[128,128]{1,0:T(8,128)S(1)} %cholesky.435), custom_call_target="Cholesky" | custom-call | tf_op jit(solution)/shard_map/jit(cholesky)/cholesky | solution.py:58
  81.4 9.8 %custom-call.33 = f32[1,128,128]{1,2,0:T(8,128)S(1)} custom-call(f32[1,128,128]{2,1,0:T(8,128)S(1)} %get-tuple-element.84), custom_call_target="InvertDiagBlocksLowerTriangular" | custom-call | tf_op jit(solution)/shard_map/jit(cholesky)/cholesky | solution.py:58
  92.6 22.2 %cholesky.343 = f32[128,128]{1,0:T(8,128)S(1)} custom-call(f32[128,128]{1,0:T(8,128)S(1)} %convolution_subtract_fusion.11), custom_call_target="Cholesky" | custom-call | tf_op jit(solution)/shard_map/jit(cholesky)/cholesky | solution.py:58
  127.4 39.3 %custom-call.34 = f32[4,128,128]{1,2,0:T(8,128)S(1)} custom-call(f32[4,128,128]{2,1,0:T(8,128)S(1)} %get-tuple-element.19), custom_call_target="InvertDiagBlocksLowerTriangular" | custom-call | tf_op jit(solution)/shard_map/triangular_solve/custom-call.3 | solution.py:59
  183.5 16.1 %fusion = f32[256,8,8,128]{3,1,2,0:T(8,128)S(1)} fusion(f32[256,8,8,128]{3,2,1,0:T(8,128)S(1)} %bitcast.224, f32[512,2048]{1,0:T(8,128)S(1)} %fusion.16, f32[512,1024]{1,0:T(8,128)S(1)} %fusion.15), kind=kOutput, calls=%fused_computation.7 | convolution fusion | flops 12886999040 | bytes 23068672 | tf_op jit(solution)/shard_map/dot_general | solution.py:66
  206.4 16.0 %gather_fusion = f32[256,128,128]{2,1,0:T(8,128)} fusion(f32[16,128,8,128]{3,1,2,0:T(8,128)} %copy.63, s32[256]{0:T(256)S(1)} %reshape.551), kind=kCustom, calls=%fused_computation | custom fusion | bytes 33556480 | tf_op jit(solution)/shard_map/gather | solution.py:115
  222.4 11.4 %broadcast_select_fusion = f32[128,2,128,128]{3,2,1,0:T(8,128)} fusion(f32[128,2,128,128]{3,2,1,0:T(8,128)} %bitcast.218, pred[128,2]{1,0:T(8,128)(4,1)S(1)} %bitcast.229), kind=kLoop, calls=%fused_computation.8 | loop fusion | flops 4194304 | bytes 33554688 | tf_op jit(solution)/shard_map/select_n | solution.py:115
  233.7 23.0 %all-to-all-start = ((f32[128,2,128,128]{3,2,1,0:T(8,128)}), f32[128,2,128,128]{3,2,1,0:T(8,128)}, u32[]{:S(2)}, u32[]{:S(2)}) async-start(f32[128,2,128,128]{3,2,1,0:T(8,128)} %broadcast_select_fusion), calls=%async_computation | async-start | bytes 33554432 | tf_op jit(solution)/shard_map/all_to_all | solution.py:116
  260.0 11.7 %cholesky.358 = f32[128,128]{1,0:T(8,128)S(1)} custom-call(f32[128,128]{1,0:T(8,128)S(1)} %cholesky.439), custom_call_target="Cholesky" | custom-call | tf_op jit(solution)/shard_map/jit(cholesky)/cholesky | solution.py:70
  284.2 11.7 %cholesky.377 = f32[128,128]{1,0:T(8,128)S(1)} custom-call(f32[128,128]{1,0:T(8,128)S(1)} %cholesky.443), custom_call_target="Cholesky" | custom-call | tf_op jit(solution)/shard_map/jit(cholesky)/cholesky | solution.py:70
  295.9 10.0 %custom-call.36 = f32[1,128,128]{1,2,0:T(8,128)S(1)} custom-call(f32[1,128,128]{2,1,0:T(8,128)S(1)} %get-tuple-element.77), custom_call_target="InvertDiagBlocksLowerTriangular" | custom-call | tf_op jit(solution)/shard_map/jit(cholesky)/cholesky | solution.py:70
  307.5 11.7 %cholesky.398 = f32[128,128]{1,0:T(8,128)S(1)} custom-call(f32[128,128]{1,0:T(8,128)S(1)} %cholesky.448), custom_call_target="Cholesky" | custom-call | tf_op jit(solution)/shard_map/jit(cholesky)/cholesky | solution.py:70
  319.2 9.8 %custom-call.37 = f32[1,128,128]{1,2,0:T(8,128)S(1)} custom-call(f32[1,128,128]{2,1,0:T(8,128)S(1)} %get-tuple-element.74), custom_call_target="InvertDiagBlocksLowerTriangular" | custom-call | tf_op jit(solution)/shard_map/jit(cholesky)/cholesky | solution.py:70
  330.5 11.7 %cholesky.415 = f32[128,128]{1,0:T(8,128)S(1)} custom-call(f32[128,128]{1,0:T(8,128)S(1)} %convolution_subtract_fusion.10), custom_call_target="Cholesky" | custom-call | tf_op jit(solution)/shard_map/jit(cholesky)/cholesky | solution.py:70
  356.7 39.3 %custom-call.38 = f32[4,128,128]{1,2,0:T(8,128)S(1)} custom-call(f32[4,128,128]{2,1,0:T(8,128)S(1)} %get-tuple-element.20), custom_call_target="InvertDiagBlocksLowerTriangular" | custom-call | tf_op jit(solution)/shard_map/triangular_solve/custom-call.3 | solution.py:71
  399.2 115.1 %all-gather.3.cloned.1.call-done = f32[24,1,1,1,128,512]{5,4,3,2,1,0:T(8,128)} async-done(((f32[24,1,1,1,8,512]{5,4,3,2,1,0:T(8,128)}), f32[24,1,1,1,128,512]{5,4,3,2,1,0:T(8,128)}) %all-gather.3.cloned.1.call-update) | async-done | bytes 6291472 | tf_op jit(solution)/shard_map/all_gather | solution.py:48
  522.8 13.8 %fusion.39 = f32[512,3072]{1,0:T(8,128)} fusion(f32[3072,512]{1,0:T(8,128)} %bitcast.221, f32[128,512]{1,0:T(8,128)S(1)} %fusion.46, f32[128,512]{1,0:T(8,128)S(1)} %fusion.47, f32[128,512]{1,0:T(8,128)S(1)} %fusion.49, f32[128,512]{1,0:T(8,128)S(1)} %fusion.26), kind=kOutput, calls=%fused_computation.75 | convolution fusion | flops 9664462848 | bytes 13631488 | tf_op jit(solution)/shard_map/dot_general | solution.py:74
  536.6 43.0 %collective-permute-done.1 = f32[4,128,512]{2,1,0:T(8,128)S(1)} collective-permute-done((f32[4,128,512]{2,1,0:T(8,128)S(1)}, f32[4,128,512]{2,1,0:T(8,128)S(1)}, u32[]{:S(2)}, u32[]{:S(2)}) %collective-permute-start.1) | collective-permute-done | bytes 1048608 | tf_op jit(solution)/shard_map/ppermute | solution.py:56
  585.0 51.7 %scatter_fusion = f32[24,128,4,128]{3,1,2,0:T(8,128)} fusion(f32[24,128,4,128]{3,1,2,0:T(8,128)} %broadcast_in_dim.69, s32[256]{0:T(256)S(1)} %reshape.559, f32[256,128,128]{2,1,0:T(8,128)} %bitcast.23), kind=kCustom, calls=%fused_computation.1 | custom fusion | flops 4194304 | bytes 50333696 | tf_op jit(solution)/shard_map/scatter-add | solution.py:126
  644.5 23.0 %bitcast_subtract_fusion.1 = f32[3072,512]{1,0:T(8,128)} fusion(f32[384,8,4,128]{3,2,1,0:T(4,128)S(1)} %bitcast.219, f32[512,3072]{1,0:T(8,128)} %fusion.39, f32[512,512]{1,0:T(8,128)S(1)} %fusion.38), kind=kOutput, calls=%fused_computation.9 | convolution fusion | flops 9665249280 | bytes 19922944 | tf_op jit(solution)/shard_map/dot_general | solution.py:78
  (175 shorter events, 132.7 us)
Async XLA Ops:
  7.2 13.6 %copy-start.1 = (f32[1,512,512]{2,1,0:T(8,128)S(1)}, f32[1,512,512]{2,1,0:T(8,128)}, u32[]{:S(2)}) copy-start(f32[1,512,512]{2,1,0:T(8,128)} %param.9) | copy-start | bytes 3145732
  10.3 167.5 %collective-permute-start = (f32[8,128,512]{2,1,0:T(8,128)}, f32[8,128,512]{2,1,0:T(8,128)}, u32[]{:S(2)}, u32[]{:S(2)}) collective-permute-start(f32[8,128,512]{2,1,0:T(8,128)} %slice_bitcast_fusion), channel_id=1, source_target_pairs={{0,0},{1,8},{2,16},{3,24},{4,32},{5,40},{6,48},{7,56},{8,1},{9,9},... | collective-permute-start | bytes 6291464 | tf_op jit(solution)/shard_map/ppermute | solution.py:45
  20.8 146.4 %copy-start.7 = (s32[2]{0:T(128)S(1)}, s32[2]{0:T(128)}, u32[]{:S(2)}) copy-start(s32[2]{0:T(128)} %constant.242.clone.1) | copy-start | bytes 28
  21.0 1.0 copy-start.3
  167.5 3.2 copy-start
  170.6 12.8 %slice-start = ((s8[8388608]{0:T(1024)(128)(4,1)}), s8[4194304]{0:T(1024)(128)(4,1)S(1)}, s32[]{:S(2)}) async-start(s8[8388608]{0:T(1024)(128)(4,1)} %bitcast.222), calls=%async_computation.2 | async-start | bytes 8388608
  170.7 12.8 %slice-start.1 = ((s8[8388608]{0:T(1024)(128)(4,1)}), s8[4194304]{0:T(1024)(128)(4,1)S(1)}, s32[]{:S(2)}) async-start(s8[8388608]{0:T(1024)(128)(4,1)} %bitcast.222), calls=%async_computation.3 | async-start | bytes 8388608
  233.7 23.7 %copy-start.6 = (s32[2,128]{1,0:T(2,128)S(1)}, s32[2,128]{1,0:T(2,128)}, u32[]{:S(2)}) copy-start(s32[2,128]{1,0:T(2,128)} %param.14) | copy-start | bytes 3076
  233.7 24.7 %copy-start.2 = (f32[512,512]{1,0:T(8,128)S(1)}, f32[512,512]{1,0:T(8,128)}, u32[]{:S(2)}) copy-start(f32[512,512]{1,0:T(8,128)} %param.12) | copy-start | bytes 3145732
  233.7 347.7 %all-to-all-start = ((f32[128,2,128,128]{3,2,1,0:T(8,128)}), f32[128,2,128,128]{3,2,1,0:T(8,128)}, u32[]{:S(2)}, u32[]{:S(2)}) async-start(f32[128,2,128,128]{3,2,1,0:T(8,128)} %broadcast_select_fusion), calls=%async_computation | async-start | bytes 33554432 | tf_op jit(solution)/shard_map/all_to_all | solution.py:116
  256.7 257.6 %all-gather.3.cloned.1.call-start = ((), (), s32[]{:S(2)}) async-start(), calls=%async_computation.1 | async-start | bytes 6684672 | tf_op jit(solution)/shard_map/all_gather | solution.py:48
  259.0 1.0 copy-start.4
  396.0 2.1 copy-start.5
  516.3 63.3 %collective-permute-start.1 = (f32[4,128,512]{2,1,0:T(8,128)S(1)}, f32[4,128,512]{2,1,0:T(8,128)S(1)}, u32[]{:S(2)}, u32[]{:S(2)}) collective-permute-start(f32[4,128,512]{2,1,0:T(8,128)S(1)} %dynamic-slice_bitcast_fusion), channel_id=1, source_target_pairs={{0,0},{1,8},{2,16},{3,24},{4,32},{5,40},{6,48},{7,56},{8,1},{9,9},... | collective-permute-start | bytes 3145736 | tf_op jit(solution)/shard_map/ppermute | solution.py:56
Sparse Core Ops, SparseCore 0:
  259.3 255.0 all-gather.2
